TPU v7x, 32 devices: a whole 2x2x4 slice. The times are simulated.
32 devices in a mesh: seq: 8 (over y, x, core), tp: 4 (over z).
Axes of the slice: x: 2, y: 2, z: 4, core: 2. Of those that a mesh axis runs over, the one named last changes fastest.
Arguments:
- hidden: bfloat16 [1024, 8192], P('seq'), may hold values from -7 to 7
- norm_gain: bfloat16 [8192], replicated, may hold values from 0.099609375 to 1.8984375
- w_query: bfloat16 [8192, 1024], P('seq', 'tp'), may hold values from -1 to 1
- w_key: bfloat16 [8192, 128], P('seq'), may hold values from -64 to 64
- w_value: bfloat16 [8192, 128], P('seq'), may hold values from -0.0625 to 0.0625
- doc_lengths: int32 [8], replicated, may hold values from 1 to 640, 1024 in all
- critic_up: bfloat16 [8192, 4608], P('seq', 'tp'), may hold values from -0.0625 to 0.0625
- critic_down: bfloat16 [4, 4608, 8192], P(None, 'tp', 'seq'), may hold values from -0.09375 to 0.09375
- rule_ids: int32 [8], replicated, may hold values from 0 to 3
Outputs:
- attention: bfloat16 [1024, 1024], P('seq', 'tp')
- critic_values: bfloat16 [8, 8192], P(None, 'seq')
Inputs may be any that keep to these rules, and one draw needn't show every extreme that they name: `doc_lengths`: the 8 lengths sum to 1024; the longest is exactly 640.
All inputs are finite; a program needn't handle non-finite values.
Results may differ from a plain program's by a relative error of at most 0.03.
The roundings to bfloat16 on the way count: a program that leaves them out, or rounds other values in their place, can miss the bound.
Values may be sent and summed in bfloat16 or wider, within the bound.
No kernel may reach another device: no remote copies, remote signals or barrier semaphores. Data moves between devices by JAX's collectives and lax.ppermute only.
A program may use at most 64 MiB of HBM per device.

v0:
```python
import math

import jax
import jax.numpy as jnp
from jax import lax
from jax.sharding import PartitionSpec as P

QH_DEV = 2
GROUP = 8


def rms_norm(values, norm_gain):
    widened = values.astype(jnp.float32)
    mean_square = jnp.mean(widened * widened, axis=-1, keepdims=True)
    return (widened * lax.rsqrt(mean_square + 1e-05) * norm_gain.astype(jnp.float32)).astype(
        jnp.bfloat16
    )


def shards(
    hidden, norm_gain, w_query, w_key, w_value, doc_lengths, critic_up, critic_down, rule_ids
):
    normed = rms_norm(hidden, norm_gain)
    tokens_here = hidden.shape[0]
    head_size = w_query.shape[1] // QH_DEV
    shared_head = lax.axis_index("tp") * QH_DEV // GROUP
    key_columns = lax.dynamic_slice_in_dim(w_key, shared_head * head_size, head_size, 1)
    value_columns = lax.dynamic_slice_in_dim(w_value, shared_head * head_size, head_size, 1)

    def project(weight_rows):
        return jnp.dot(normed, weight_rows, preferred_element_type=jnp.float32)

    query_sum = project(lax.all_gather(w_query, "seq", axis=0, tiled=True))
    key_sum = project(lax.all_gather(key_columns, "seq", axis=0, tiled=True))
    value_sum = project(lax.all_gather(value_columns, "seq", axis=0, tiled=True))
    queries = query_sum.astype(jnp.bfloat16).reshape(tokens_here, QH_DEV, head_size)
    keys = key_sum.astype(jnp.bfloat16)
    values = value_sum.astype(jnp.bfloat16)
    doc_ends = jnp.cumsum(doc_lengths) - 1
    first_row = lax.axis_index("seq") * tokens_here
    query_pos = first_row + jnp.arange(tokens_here, dtype=jnp.int32)

    def segment_of(positions):
        return jnp.sum((positions[:, None] > doc_ends[None, :]).astype(jnp.int32), axis=1)

    query_seg = segment_of(query_pos)
    inverse_root = 1.0 / math.sqrt(head_size)
    maxima = jnp.full((tokens_here, QH_DEV), -1e30, jnp.float32)
    key_block = lax.all_gather(keys, "seq", axis=0, tiled=True)
    value_block = lax.all_gather(values, "seq", axis=0, tiled=True)
    key_pos = jnp.arange(key_block.shape[0], dtype=jnp.int32)
    allowed = (query_seg[:, None] == segment_of(key_pos)[None, :]) & (
        key_pos[None, :] <= query_pos[:, None]
    )
    allowed = allowed[:, None, :]
    scores = (
        jnp.einsum("qhd,kd->qhk", queries, key_block, preferred_element_type=jnp.float32)
        * inverse_root
    )
    scores = jnp.where(allowed, scores, -1e30)
    new_max = jnp.maximum(maxima, jnp.max(scores, axis=2))
    expanded = jnp.where(allowed, jnp.exp(scores - new_max[:, :, None]), 0.0)
    totals = jnp.sum(expanded, axis=2)
    weighted = jnp.einsum(
        "qhk,kd->qhd",
        expanded.astype(jnp.bfloat16),
        value_block,
        preferred_element_type=jnp.float32,
    )
    maxima, totals, weighted = (new_max, totals, weighted)
    attention = (
        (weighted / totals[:, :, None])
        .reshape(tokens_here, QH_DEV * head_size)
        .astype(jnp.bfloat16)
    )
    picker = (doc_ends[:, None] == query_pos[None, :]).astype(jnp.bfloat16)
    end_terms = jnp.dot(picker, normed, preferred_element_type=jnp.float32)
    end_rows = lax.psum_scatter(
        end_terms.astype(jnp.bfloat16), "seq", scatter_dimension=1, tiled=True
    )
    up_terms = jnp.dot(end_rows, critic_up, preferred_element_type=jnp.float32)
    critic_hidden = jax.nn.silu(
        lax.psum(up_terms.astype(jnp.bfloat16), "seq").astype(jnp.float32)
    ).astype(jnp.bfloat16)
    per_rule = jnp.einsum(
        "dc,rce->dre", critic_hidden, critic_down, preferred_element_type=jnp.float32
    )
    rule_pick = (
        rule_ids[:, None] == jnp.arange(critic_down.shape[0], dtype=jnp.int32)[None, :]
    ).astype(jnp.float32)
    chosen = jnp.einsum("dr,dre->de", rule_pick, per_rule)
    critic_values = lax.psum(chosen, "tp").astype(jnp.bfloat16)
    return (attention, critic_values)


def solution(mesh):
    return jax.shard_map(
        shards,
        mesh=mesh,
        in_specs=(
            P("seq", None),
            P(),
            P("seq", "tp"),
            P("seq", None),
            P("seq", None),
            P(),
            P("seq", "tp"),
            P(None, "tp", "seq"),
            P(),
        ),
        out_specs=(P("seq", "tp"), P(None, "seq")),
        check_vma=False,
    )
```

profile of v0, /device:TPU:0, one launch (start us, length us, event | category | flops | bytes accessed | tf_op | source)
XLA Modules:
  0.0 161.3 jit_solution(6691968196375162976)
XLA Ops:
  7.2 0.0 copy-start
  7.2 0.0 copy-start.1
  7.2 0.0 reduce-scatter.2.cloned.1.call-start
  7.2 0.9 convert_element_type.53
  8.1 2.1 %fusion = f32[128]{0:T(128)S(1)} fusion(bf16[128,8192]{1,0:T(8,128)(2,1)} %param.9), kind=kLoop, calls=%fused_computation.3 | loop fusion | flops 3145600 | bytes 2097664 | tf_op jit(solution)/shard_map/reduce_sum | solution.py:14
  10.2 0.8 reduce-window.7
  11.1 2.9 %convolution_convert_fusion = bf16[8,8192]{1,0:T(8,128)(2,1)} fusion(s32[128]{0:T(128)S(1)} %iota_add_fusion, s32[8]{0:T(128)S(1)} %add_bitcast_fusion, bf16[128,8192]{1,0:T(8,128)(2,1)} %param.9, f32[8192]{0:T(1024)S(1)} %convert_element_type.53, f32[128]{0:T(128)S(1)} %add_rsqrt_fusion), kind=kOutput, calls=%fused_computation | convolution fusion | flops 21038080 | bytes 2262048 | tf_op jit(solution)/shard_map/dot_general | solution.py:77
  14.0 0.0 reduce-scatter.2.cloned.1.call-update
  14.0 0.0 all-gather.6.cloned.1.call-start
  14.0 0.7 all-gather.6.cloned.1.call-update
  14.7 0.0 all-gather.8.cloned.1.call-start
  14.8 0.7 all-gather.8.cloned.1.call-update
  15.5 0.0 all-gather.4.cloned.1.call-start
  15.5 0.5 all-gather.4.cloned.1.call-update
  16.0 0.1 convert_reduce_fusion
  16.1 0.1 convert_reduce_fusion.1
  16.2 0.0 copy-done.1
  16.2 0.1 fusion.28
  16.3 0.2 fusion.11
  16.5 33.9 %reduce-scatter.2.cloned.1.call-done = bf16[8,1024]{1,0:T(8,128)(2,1)} async-done(((bf16[8,8192]{1,0:T(8,128)(2,1)}), bf16[8,1024]{1,0:T(8,128)(2,1)}) %reduce-scatter.2.cloned.1.call-update) | async-done | bytes 16400 | tf_op jit(solution)/shard_map/reduce_scatter | solution.py:78
  50.4 0.0 copy-done
  50.4 1.1 convolution_convert_fusion.1
  51.5 22.8 %psum.14 = bf16[8,1152]{1,0:T(8,128)(2,1)S(1)} all-reduce(bf16[8,1152]{1,0:T(8,128)(2,1)S(1)} %convolution_convert_fusion.1), channel_id=1, replica_groups=mesh['seq'=8,'tp'=4] {'seq'}, use_global_device_ids=true, to_apply=%region_7.8 | all-reduce | flops 9216 | bytes 36864 | tf_op jit(solution)/shard_map/psum | solution.py:83
  74.3 5.1 %fusion.24 = bf16[8,4,1024]{2,0,1:T(8,128)(2,1)S(1)} fusion(bf16[4,1152,1024]{2,1,0:T(8,128)(2,1)} %param.16, bf16[8,1152]{1,0:T(8,128)(2,1)S(1)} %psum.14), kind=kOutput, calls=%fused_computation.39 | convolution fusion | flops 75552768 | bytes 9521152 | tf_op jit(solution)/shard_map/dc,rce->dre/dot_general | solution.py:85
  79.4 0.2 fusion.15
  79.6 19.6 %psum.15 = bf16[8,1024]{1,0:T(8,128)(2,1)} all-reduce(f32[8,1024]{1,0:T(8,128)S(1)} %bitcast.33), channel_id=1, replica_groups=mesh['seq'=8,'tp'=4] {'tp'}, use_global_device_ids=true, to_apply=%region_8.9 | all-reduce | flops 8192 | bytes 49152 | tf_op jit(solution)/shard_map/psum | solution.py:92
  99.2 0.0 all-gather.6.cloned.1.call-done
  99.2 3.4 %convolution_convert_fusion.4 = bf16[128,128]{1,0:T(8,128)(2,1)S(1)} fusion(bf16[8192,128]{1,0:T(8,128)(2,1)} %all-gather.6.cloned.1.call-done, bf16[128,8192]{1,0:T(8,128)(2,1)} %param.9, f32[8192]{0:T(1024)S(1)} %convert_element_type.53, f32[128]{0:T(128)S(1)} %add_rsqrt_fusion), kind=kOutput, calls=%fused_computation.14 | convolution fusion | flops 272646144 | bytes 4260352 | tf_op jit(solution)/shard_map/dot_general | solution.py:31
  102.5 9.8 %all_gather.17 = bf16[1024,128]{1,0:T(8,128)(2,1)S(1)} all-gather(bf16[128,128]{1,0:T(8,128)(2,1)S(1)} %convolution_convert_fusion.4), channel_id=1, replica_groups=mesh['seq'=8,'tp'=4] {'seq'}, dimensions={0}, use_global_device_ids=true | all-gather | bytes 294912 | tf_op jit(solution)/shard_map/all_gather | solution.py:49
  112.4 0.0 all-gather.8.cloned.1.call-done
  112.4 3.3 %convolution_convert_fusion.3 = bf16[128,128]{0,1:T(8,128)(2,1)S(1)} fusion(bf16[8192,128]{1,0:T(8,128)(2,1)} %all-gather.8.cloned.1.call-done, bf16[128,8192]{1,0:T(8,128)(2,1)} %param.9, f32[8192]{0:T(1024)S(1)} %convert_element_type.53, f32[128]{0:T(128)S(1)} %add_rsqrt_fusion), kind=kOutput, calls=%fused_computation.13 | convolution fusion | flops 272646144 | bytes 4260352 | tf_op jit(solution)/shard_map/dot_general | solution.py:31
  115.7 8.8 %all_gather.19 = bf16[1024,128]{0,1:T(8,128)(2,1)S(1)} all-gather(bf16[128,128]{0,1:T(8,128)(2,1)S(1)} %convolution_convert_fusion.3), channel_id=1, replica_groups=mesh['seq'=8,'tp'=4] {'seq'}, dimensions={0}, use_global_device_ids=true | all-gather | bytes 294912 | tf_op jit(solution)/shard_map/all_gather | solution.py:50
  124.5 24.7 %all-gather.4.cloned.1.call-done = bf16[8192,256]{1,0:T(8,128)(2,1)} async-done(((bf16[1024,256]{1,0:T(8,128)(2,1)}), bf16[8192,256]{1,0:T(8,128)(2,1)}) %all-gather.4.cloned.1.call-update) | async-done | bytes 4194320 | tf_op jit(solution)/shard_map/all_gather | solution.py:33
  149.2 3.6 %fusion.5 = bf16[16,2,8,128]{3,2,1,0:T(8,128)(2,1)S(1)} fusion(bf16[8192,256]{1,0:T(8,128)(2,1)} %all-gather.4.cloned.1.call-done, bf16[128,8192]{1,0:T(8,128)(2,1)} %param.9, f32[8192]{0:T(1024)S(1)} %convert_element_type.53, f32[128]{0:T(128)S(1)} %add_rsqrt_fusion), kind=kOutput, calls=%fused_computation.12 | convolution fusion | flops 541097984 | bytes 6390272 | tf_op jit(solution)/shard_map/dot_general | solution.py:31
  152.8 0.4 fusion.38
  153.2 0.4 fusion.6
  153.6 0.5 fusion.4
  154.1 0.7 copy.14
  (5 shorter events, 0.0 us)
Async XLA Ops:
  7.2 43.3 %copy-start = (bf16[1024,1152]{1,0:T(8,128)(2,1)S(1)}, bf16[1024,1152]{1,0:T(8,128)(2,1)}, u32[]{:S(2)}) copy-start(bf16[1024,1152]{1,0:T(8,128)(2,1)} %param.15) | copy-start | bytes 7077892
  7.2 9.0 %copy-start.1 = (s32[8]{0:T(128)S(1)}, s32[8]{0:T(128)}, u32[]{:S(2)}) copy-start(s32[8]{0:T(128)} %param.17) | copy-start | bytes 100
  7.2 43.2 %reduce-scatter.2.cloned.1.call-start = ((), (), s32[]{:S(2)}) async-start(), calls=%async_computation.4 | async-start | bytes 147456 | tf_op jit(solution)/shard_map/reduce_scatter | solution.py:78
  14.0 85.2 %all-gather.6.cloned.1.call-start = ((), (), s32[]{:S(2)}) async-start(), calls=%async_computation.2 | async-start | bytes 2359296 | tf_op jit(solution)/shard_map/all_gather | solution.py:34
  14.7 97.6 %all-gather.8.cloned.1.call-start = ((), (), s32[]{:S(2)}) async-start(), calls=%async_computation.3 | async-start | bytes 2359296 | tf_op jit(solution)/shard_map/all_gather | solution.py:35
  15.5 133.7 %all-gather.4.cloned.1.call-start = ((), (), s32[]{:S(2)}) async-start(), calls=%async_computation.1 | async-start | bytes 4718592 | tf_op jit(solution)/shard_map/all_gather | solution.py:33
Sparse Core Ops, SparseCore 0:
  14.1 36.2 reduce-scatter.1
  52.3 27.8 all-gather.5
  82.1 28.0 all-gather.7
  111.9 37.2 all-gather.3
where the time goes:
time: 162 us; the launch traced here: 161 us
  blocking collectives  61 us (38%)
  waiting for transfers between devices  60.5 us (37%)
  matrix products  20.5 us (13%)
  between operations  13.9 us (9%)
  other arithmetic  4.61 us (3%)
    reduce_scatter x1, waiting for transfers between devices, shards(): lax.psum_scatter(end_terms.astype(jnp.bfloat16), 'seq', scatter_dimension...  33.9 us
    all_gather x1, waiting for transfers between devices, shards(): query_sum = project(lax.all_gather(w_query, 'seq', axis=0, tiled=True))  24.7 us
    psum x1, blocking collectives, shards(): lax.psum(up_terms.astype(jnp.bfloat16), 'seq').astype(jnp.float32)  22.8 us
    psum x1, blocking collectives, shards(): critic_values = lax.psum(chosen, 'tp').astype(jnp.bfloat16)  19.6 us
    dot_general x3, matrix products, project(): return jnp.dot(normed, weight_rows, preferred_element_type=jnp.float32)  10.3 us
    all_gather x1, blocking collectives, shards(): key_block = lax.all_gather(keys, 'seq', axis=0, tiled=True)  9.83 us
    all_gather x1, blocking collectives, shards(): value_block = lax.all_gather(values, 'seq', axis=0, tiled=True)  8.84 us
    dot_general x1, matrix products, shards(): jnp.einsum('dc,rce->dre', critic_hidden, critic_down, preferred_element_t...  5.09 us
  transfers between devices with their start and end apart: 4, of which 2 were waited for; matrix products, arithmetic and copies ran while one was open for 8% of the time, Pallas kernels for 0%

commit v1 on v0

v1 whole, which is shorter than its diff:
```python
import math

import jax
import jax.numpy as jnp
from jax import lax
from jax.sharding import PartitionSpec as P

HEAD = 128
GROUP = 8


def rms_norm(values, norm_gain):
    widened = values.astype(jnp.float32)
    mean_square = jnp.mean(widened * widened, axis=-1, keepdims=True)
    return (widened * lax.rsqrt(mean_square + 1e-05) * norm_gain.astype(jnp.float32)).astype(
        jnp.bfloat16
    )


def shifted(x, axis, n, k):
    return lax.ppermute(x, axis, [(j, (j + k) % n) for j in range(n)])


def group_shifted(x, axis, n, size, k):
    perm = [(j, j - j % size + (j % size + k) % size) for j in range(n)]
    return lax.ppermute(x, axis, perm)


def xor_perm(n, pick):
    return [(j, pick(j)) for j in range(n)]


def gather_pieces(blk, n):
    i = lax.axis_index("seq")
    rows = blk.shape[0]
    if n != 8:
        full = lax.all_gather(blk, "seq", axis=0, tiled=True)
        return [(full, jnp.int32(0), n * rows)]
    core = i % 2
    chip = i // 2
    sib = lax.ppermute(blk, "seq", xor_perm(8, lambda j: j ^ 1))
    pair = jnp.concatenate([blk, sib], axis=0)
    nb = lax.ppermute(pair, "seq", xor_perm(8, lambda j: j ^ 2 if j % 2 == 0 else j ^ 4))
    dg = lax.ppermute(nb[:rows], "seq", xor_perm(8, lambda j: j ^ 5 if j % 2 == 0 else j ^ 3))
    oth = lax.ppermute(jnp.concatenate([nb, dg], axis=0), "seq", xor_perm(8, lambda j: j ^ 1))
    nb_chip = chip ^ (1 + core)
    oth_chip = chip ^ (2 - core)
    diag = chip ^ 3
    return [
        (blk, i, rows),
        (sib, i ^ 1, rows),
        (nb[:rows], 2 * nb_chip + core, rows),
        (nb[rows:], 2 * nb_chip + 1 - core, rows),
        (dg, 2 * diag + 1 - core, rows),
        (oth[:rows], 2 * oth_chip + 1 - core, rows),
        (oth[rows : 2 * rows], 2 * oth_chip + core, rows),
        (oth[2 * rows :], 2 * diag + core, rows),
    ]


def project(normed, pieces):
    total = None
    for piece, source, rows in pieces:
        cols = lax.dynamic_slice_in_dim(normed, source * rows, rows, 1)
        term = jnp.dot(cols, piece, preferred_element_type=jnp.float32)
        total = term if total is None else total + term
    return total


def shards(
    hidden, norm_gain, w_query, w_key, w_value, doc_lengths, critic_up, critic_down, rule_ids
):
    n_seq = lax.axis_size("seq")
    n_tp = lax.axis_size("tp")
    seq_i = lax.axis_index("seq")
    tp_i = lax.axis_index("tp")
    normed = rms_norm(hidden, norm_gain)
    tokens_here = hidden.shape[0]
    d_rows = w_query.shape[0]
    heads_here = w_query.shape[1] // HEAD
    sharers = GROUP // heads_here
    kv_width = HEAD // sharers
    kv_head = tp_i * heads_here // GROUP
    kv_part = tp_i % sharers
    kv_start = kv_head * HEAD + kv_part * kv_width
    key_cols = lax.dynamic_slice_in_dim(w_key, kv_start, kv_width, 1)
    value_cols = lax.dynamic_slice_in_dim(w_value, kv_start, kv_width, 1)
    kv_weights = jnp.concatenate([key_cols, value_cols], axis=1)

    doc_ends = jnp.cumsum(doc_lengths) - 1
    first_row = seq_i * tokens_here
    query_pos = first_row + jnp.arange(tokens_here, dtype=jnp.int32)
    picker = (doc_ends[:, None] == query_pos[None, :]).astype(jnp.bfloat16)
    end_terms = jnp.dot(picker, normed, preferred_element_type=jnp.float32).astype(jnp.bfloat16)
    end_sum = lax.dynamic_slice_in_dim(end_terms, seq_i * d_rows, d_rows, 1).astype(jnp.float32)
    for k in range(1, n_seq):
        part = lax.dynamic_slice_in_dim(end_terms, ((seq_i + k) % n_seq) * d_rows, d_rows, 1)
        end_sum = end_sum + shifted(part, "seq", n_seq, k).astype(jnp.float32)
    end_rows = end_sum.astype(jnp.bfloat16)
    up_own = jnp.dot(end_rows, critic_up, preferred_element_type=jnp.float32)
    up_sum = up_own
    for k in range(1, n_seq):
        up_sum = up_sum + shifted(up_own, "seq", n_seq, k)
    critic_hidden = jax.nn.silu(up_sum).astype(jnp.bfloat16)
    per_rule = jnp.einsum(
        "dc,rce->dre", critic_hidden, critic_down, preferred_element_type=jnp.float32
    )
    rule_pick = rule_ids[:, None] == jnp.arange(critic_down.shape[0], dtype=jnp.int32)[None, :]
    chosen = jnp.sum(jnp.where(rule_pick[:, :, None], per_rule, 0.0), axis=1)
    if n_tp > 8:
        critic_sum = lax.psum(chosen, "tp")
    else:
        received = [chosen] + [shifted(chosen, "tp", n_tp, k) for k in range(1, n_tp)]
        critic_sum = None
        for m in range(n_tp):
            canon = received[0]
            for k in range(1, n_tp):
                canon = jnp.where((tp_i - k) % n_tp == m, received[k], canon)
            critic_sum = canon if critic_sum is None else critic_sum + canon
    critic_values = critic_sum.astype(jnp.bfloat16)

    kv_pieces = gather_pieces(kv_weights, n_seq)
    kv_own = project(normed, kv_pieces).astype(jnp.bfloat16)
    kv_got = [kv_own] + [group_shifted(kv_own, "tp", n_tp, sharers, k) for k in range(1, sharers)]
    key_parts, value_parts = [], []
    for m in range(sharers):
        canon = kv_got[0]
        for k in range(1, sharers):
            canon = jnp.where((kv_part - k) % sharers == m, kv_got[k], canon)
        key_parts.append(canon[:, :kv_width])
        value_parts.append(canon[:, kv_width:])
    kv_rows = jnp.concatenate(key_parts + value_parts, axis=1)
    kv_all = [kv_rows] + [shifted(kv_rows, "seq", n_seq, k) for k in range(1, n_seq)]
    key_block = jnp.concatenate([piece[:, :HEAD] for piece in kv_all], axis=0)
    value_block = jnp.concatenate([piece[:, HEAD:] for piece in kv_all], axis=0)
    key_pos = jnp.concatenate(
        [
            ((seq_i - k) % n_seq) * tokens_here + jnp.arange(tokens_here, dtype=jnp.int32)
            for k in range(n_seq)
        ]
    )

    q_pieces = gather_pieces(w_query, n_seq)
    queries = project(normed, q_pieces).astype(jnp.bfloat16).reshape(tokens_here, heads_here, HEAD)

    def segment_of(positions):
        return jnp.sum((positions[:, None] > doc_ends[None, :]).astype(jnp.int32), axis=1)

    query_seg = segment_of(query_pos)
    inverse_root = 1.0 / math.sqrt(HEAD)
    allowed = (query_seg[:, None] == segment_of(key_pos)[None, :]) & (
        key_pos[None, :] <= query_pos[:, None]
    )
    allowed = allowed[:, None, :]
    scores = (
        jnp.einsum("qhd,kd->qhk", queries, key_block, preferred_element_type=jnp.float32)
        * inverse_root
    )
    scores = jnp.where(allowed, scores, -1e30)
    maxima = jnp.max(scores, axis=2)
    expanded = jnp.where(allowed, jnp.exp(scores - maxima[:, :, None]), 0.0)
    totals = jnp.sum(expanded, axis=2)
    weighted = jnp.einsum(
        "qhk,kd->qhd",
        expanded.astype(jnp.bfloat16),
        value_block,
        preferred_element_type=jnp.float32,
    )
    attention = (
        (weighted / totals[:, :, None])
        .reshape(tokens_here, heads_here * HEAD)
        .astype(jnp.bfloat16)
    )
    return (attention, critic_values)


def solution(mesh):
    return jax.shard_map(
        shards,
        mesh=mesh,
        in_specs=(
            P("seq", None),
            P(),
            P("seq", "tp"),
            P("seq", None),
            P("seq", None),
            P(),
            P("seq", "tp"),
            P(None, "tp", "seq"),
            P(),
        ),
        out_specs=(P("seq", "tp"), P(None, "seq")),
        check_vma=False,
    )
```

time: 162 us -> 102 us (0.63)
  blocking collectives: 61 us -> 0 us
  starting transfers between devices: 0.16 us -> 32.7 us
  waiting for transfers between devices: 60.5 us -> 36.1 us
  between operations: 13.9 us -> 1.78 us
  local copies, waits for them, and re-layouts: 0.77 us -> 6.57 us
  matrix products: 20.5 us -> 16.8 us
  other arithmetic: 4.61 us -> 7.59 us
    psum x2 -> x0, blocking collectives: 42.3 us -> none  [the longest x1 22.8 us: shards(): lax.psum(up_terms.astype(jnp.bfloat16), 'seq').astype(jnp.float32)]
    ppermute x0 -> x35, waiting for transfers between devices: none -> 36.1 us  [the longest x24 14.6 us: shifted(): return lax.ppermute(x, axis, [(j, (j + k) % n) for j in range(n)])]
    reduce_scatter x1 -> x0, waiting for transfers between devices: 33.9 us -> none  [shards(): lax.psum_scatter(end_terms.astype(jnp.bfloat16), 'seq', scatter_dimension...]
    ppermute x0 -> x35, starting transfers between devices: none -> 32.7 us  [the longest x24 25.5 us: shifted(): return lax.ppermute(x, axis, [(j, (j + k) % n) for j in range(n)])]
    all_gather x3 -> x0, waiting for transfers between devices: 24.7 us -> none  [the longest x1 24.7 us: shards(): query_sum = project(lax.all_gather(w_query, 'seq', axis=0, tiled=True))]
    all_gather x2 -> x0, blocking collectives: 18.7 us -> none  [the longest x1 9.83 us: shards(): key_block = lax.all_gather(keys, 'seq', axis=0, tiled=True)]
    dot_general x6 -> x18, matrix products: 14.5 us -> 7.8 us  [the longest x16 6.15 us: project(): term = jnp.dot(cols, piece, preferred_element_type=jnp.float32)]
    unnamed x5 -> x38, local copies, waits for them, and re-layouts: 0.76 us -> 4.6 us
  transfers between devices with their start and end apart: 4 -> 35, of which waited for: 2 -> 15; matrix products, arithmetic and copies ran while one was open for 8% -> 14% of each run, Pallas kernels for 0% -> 0%
where the time goes in v1:
time: 102 us
  waiting for transfers between devices  36.1 us (35%)
  starting transfers between devices  32.7 us (32%)
  matrix products  16.8 us (16%)
  other arithmetic  7.59 us (7%)
  local copies, waits for them, and re-layouts  6.57 us (6%)
  between operations  1.78 us (2%)
    ppermute x24, starting transfers between devices, shifted(): return lax.ppermute(x, axis, [(j, (j + k) % n) for j in range(n)])  25.5 us
    ppermute x24, waiting for transfers between devices, shifted(): return lax.ppermute(x, axis, [(j, (j + k) % n) for j in range(n)])  14.6 us
    ppermute x2, waiting for transfers between devices, gather_pieces(): lax.ppermute(pair, 'seq', xor_perm(8, lambda j: j ^ 2 if j % 2 == 0 else...  9.01 us
    ppermute x2, waiting for transfers between devices, gather_pieces(): lax.ppermute(nb[:rows], 'seq', xor_perm(8, lambda j: j ^ 5 if j % 2 == 0...  6.89 us
    dot_general x16, matrix products, project(): term = jnp.dot(cols, piece, preferred_element_type=jnp.float32)  6.15 us
    dot_general x1, matrix products, shards(): jnp.einsum('dc,rce->dre', critic_hidden, critic_down, preferred_element_t...  5.03 us
    unnamed x38, local copies, waits for them, and re-layouts  4.6 us
    ppermute x3, starting transfers between devices, group_shifted(): return lax.ppermute(x, axis, perm)  3.88 us
  transfers between devices with their start and end apart: 35, of which 15 were waited for; matrix products, arithmetic and copies ran while one was open for 14% of the time, Pallas kernels for 0%

profile of v1, /device:TPU:0, one launch (start us, length us, event | category | flops | bytes accessed | tf_op | source)
XLA Modules:
  0.0 101.6 jit_solution(11493970960542331968)
XLA Ops:
  1.0 0.8 reduce-window.7
  1.8 2.1 %fusion.1 = f32[128]{0:T(128)S(1)} fusion(bf16[128,8192]{1,0:T(8,128)(2,1)} %param.9), kind=kLoop, calls=%fused_computation.4 | loop fusion | flops 3145600 | bytes 2097664 | tf_op jit(solution)/shard_map/reduce_sum | solution.py:14
  4.1 2.2 %fusion.3 = bf16[128,8192]{1,0:T(8,128)(2,1)S(1)} fusion(bf16[128,8192]{1,0:T(8,128)(2,1)} %param.9, f32[8192]{0:T(1024)S(1)} %convert_element_type.70, f32[128]{0:T(128)S(1)} %add_rsqrt_fusion), kind=kLoop, calls=%fused_computation.6 | loop fusion | flops 4194304 | bytes 4227584 | tf_op jit(solution)/shard_map/convert_element_type | solution.py:15
  6.3 1.3 %copy-done.1 = bf16[128,8192]{1,0:T(8,128)(2,1)} copy-done((bf16[128,8192]{1,0:T(8,128)(2,1)}, bf16[128,8192]{1,0:T(8,128)(2,1)S(1)}, u32[]{:S(2)}) %copy-start.1) | copy-done | bytes 2097176
  7.6 0.4 convolution_convert_fusion
  8.0 0.7 copy-done.4
  8.7 0.6 constant_dynamic-slice_fusion.6
  9.3 0.5 collective-permute-start.18
  9.8 2.9 %collective-permute-start.24 = (bf16[8,1024]{1,0:T(8,128)(2,1)S(1)}, bf16[8,1024]{1,0:T(8,128)(2,1)S(1)}, u32[]{:S(2)}, u32[]{:S(2)}) collective-permute-start(bf16[8,1024]{1,0:T(8,128)(2,1)S(1)} %get-tuple-element.9), channel_id=1, source_target_pairs={{0,28},{4,0},{8,4},{12,8},{16,12},{20,16},{24,20},{28,24},{1,29},{... | collective-permute-start | bytes 49160 | tf_op jit(solution)/shard_map/ppermute | solution.py:21
  12.7 2.3 %collective-permute-start.23 = (bf16[8,1024]{1,0:T(8,128)(2,1)}, bf16[8,1024]{1,0:T(8,128)(2,1)}, u32[]{:S(2)}, u32[]{:S(2)}) collective-permute-start(bf16[8,1024]{1,0:T(8,128)(2,1)} %get-tuple-element.10), channel_id=1, source_target_pairs={{0,24},{4,28},{8,0},{12,4},{16,8},{20,12},{24,16},{28,20},{1,25},{... | collective-permute-start | bytes 49160 | tf_op jit(solution)/shard_map/ppermute | solution.py:21
  15.0 0.5 collective-permute-start.21
  15.7 0.8 compare_and_fusion
  16.5 1.8 %fusion.56 = f32[128,256]{1,0:T(8,128)} fusion(bf16[1024,256]{1,0:T(8,128)(2,1)S(1)} %copy-done.3, bf16[128,8192]{1,0:T(8,128)(2,1)} %copy-done.1, s32[]{:T(128)S(6)} %select_n.366), kind=kOutput, calls=%fused_computation.71 | convolution fusion | flops 67108864 | bytes 917508 | tf_op jit(solution)/shard_map/dot_general | solution.py:65
  18.3 0.5 iota_compare_fusion
  18.9 1.5 %collective-permute-start.20 = (bf16[8,1024]{1,0:T(8,128)(2,1)}, bf16[8,1024]{1,0:T(8,128)(2,1)}, u32[]{:S(2)}, u32[]{:S(2)}) collective-permute-start(bf16[8,1024]{1,0:T(8,128)(2,1)} %get-tuple-element.13), channel_id=1, source_target_pairs={{0,12},{4,16},{8,20},{12,24},{16,28},{20,0},{24,4},{28,8},{1,13},{... | collective-permute-start | bytes 49160 | tf_op jit(solution)/shard_map/ppermute | solution.py:21
  20.3 2.4 %collective-permute-start.19 = (bf16[8,1024]{1,0:T(8,128)(2,1)}, bf16[8,1024]{1,0:T(8,128)(2,1)}, u32[]{:S(2)}, u32[]{:S(2)}) collective-permute-start(bf16[8,1024]{1,0:T(8,128)(2,1)} %get-tuple-element.14), channel_id=1, source_target_pairs={{0,8},{4,12},{8,16},{12,20},{16,24},{20,28},{24,0},{28,4},{1,9},{5... | collective-permute-start | bytes 49160 | tf_op jit(solution)/shard_map/ppermute | solution.py:21
  22.7 1.2 %constant_dynamic-slice_fusion.7 = (bf16[1024,32]{1,0:T(8,128)(2,1)S(1)}, bf16[1024,32]{1,0:T(8,128)(2,1)S(1)}) fusion(bf16[1024,128]{1,0:T(8,128)(2,1)} %param.13, s32[]{:T(128)S(6)} %select_n.380, bf16[1024,128]{1,0:T(8,128)(2,1)} %param.12), kind=kLoop, calls=%fused_computation.141 | loop fusion | bytes 262148 | tf_op jit(solution)/shard_map/dynamic_slice | solution.py:87
  24.3 1.0 %collective-permute-done.19 = bf16[8,1024]{1,0:T(8,128)(2,1)} collective-permute-done((bf16[8,1024]{1,0:T(8,128)(2,1)}, bf16[8,1024]{1,0:T(8,128)(2,1)}, u32[]{:S(2)}, u32[]{:S(2)}) %collective-permute-start.19) | collective-permute-done | bytes 16416 | tf_op jit(solution)/shard_map/ppermute | solution.py:21
  25.3 1.2 %fusion.71 = f32[8,1152]{1,0:T(8,128)S(1)} fusion(bf16[1024,1152]{1,0:T(8,128)(2,1)S(1)} %copy-done, bf16[8,1024]{1,0:T(8,128)(2,1)} %copy-done.9, bf16[8,1024]{1,0:T(8,128)(2,1)} %collective-permute-done.23, bf16[8,1024]{1,0:T(8,128)(2,1)} %collective-permute-done.22, bf16[8,1024]{1,0:T(8,128)(2,1)} %collective-permute-done.21, ...), kind=kOutput, calls=%fused_computation.112 | convolution fusion | flops 19005440 | bytes 2527236 | tf_op jit(solution)/shard_map/dot_general | solution.py:100
  26.6 1.8 %collective-permute-start.30 = (f32[8,1152]{1,0:T(8,128)S(1)}, f32[8,1152]{1,0:T(8,128)S(1)}, u32[]{:S(2)}, u32[]{:S(2)}) collective-permute-start(f32[8,1152]{1,0:T(8,128)S(1)} %fusion.71), channel_id=1, source_target_pairs={{0,24},{4,28},{8,0},{12,4},{16,8},{20,12},{24,16},{28,20},{1,25},{... | collective-permute-start | bytes 110600 | tf_op jit(solution)/shard_map/ppermute | solution.py:21
  28.4 1.0 %collective-permute-start.29 = (f32[8,1152]{1,0:T(8,128)S(1)}, f32[8,1152]{1,0:T(8,128)S(1)}, u32[]{:S(2)}, u32[]{:S(2)}) collective-permute-start(f32[8,1152]{1,0:T(8,128)S(1)} %fusion.71), channel_id=1, source_target_pairs={{0,20},{4,24},{8,28},{12,0},{16,4},{20,8},{24,12},{28,16},{1,21},{... | collective-permute-start | bytes 110600 | tf_op jit(solution)/shard_map/ppermute | solution.py:21
  29.4 0.3 collective-permute-start.28
  29.7 1.4 %collective-permute-start.27 = (f32[8,1152]{1,0:T(8,128)S(1)}, f32[8,1152]{1,0:T(8,128)S(1)}, u32[]{:S(2)}, u32[]{:S(2)}) collective-permute-start(f32[8,1152]{1,0:T(8,128)S(1)} %fusion.71), channel_id=1, source_target_pairs={{0,12},{4,16},{8,20},{12,24},{16,28},{20,0},{24,4},{28,8},{1,13},{... | collective-permute-start | bytes 110600 | tf_op jit(solution)/shard_map/ppermute | solution.py:21
  31.1 1.5 %collective-permute-start.26 = (f32[8,1152]{1,0:T(8,128)S(1)}, f32[8,1152]{1,0:T(8,128)S(1)}, u32[]{:S(2)}, u32[]{:S(2)}) collective-permute-start(f32[8,1152]{1,0:T(8,128)S(1)} %fusion.71), channel_id=1, source_target_pairs={{0,8},{4,12},{8,16},{12,20},{16,24},{20,28},{24,0},{28,4},{1,9},{5... | collective-permute-start | bytes 110600 | tf_op jit(solution)/shard_map/ppermute | solution.py:21
  32.6 1.2 %fusion.54 = f32[128,64]{0,1:T(8,128)S(1)} fusion(bf16[128,8192]{1,0:T(8,128)(2,1)} %copy-done.1, s32[]{:T(128)S(6)} %select_n.366, bf16[1024,32]{0,1:T(8,128)(2,1)S(1)} %copy.27, bf16[1024,32]{0,1:T(8,128)(2,1)S(1)} %copy.26), kind=kOutput, calls=%fused_computation.69 | convolution fusion | flops 17039360 | bytes 425988 | tf_op jit(solution)/shard_map/dot_general | solution.py:65
  34.0 1.0 collective-permute-start
  35.1 0.9 collective-permute-done.26
  36.0 0.9 collective-permute-done.25
  36.9 5.0 %fusion.15 = f32[8,1024]{1,0:T(8,128)S(1)} fusion(bf16[4,1152,1024]{2,1,0:T(8,128)(2,1)} %param.16, pred[8,4]{0,1:T(4,128)(4,1)} %iota_compare_fusion, f32[8,1152]{1,0:T(8,128)S(1)} %collective-permute-done.31, f32[8,1152]{1,0:T(8,128)S(1)} %collective-permute-done.30, f32[8,1152]{1,0:T(8,128)S(1)} %collective-permute-done.29, ...), kind=kOutput, calls=%fused_computation.24 | convolution fusion | flops 75665408 | bytes 9764896 | tf_op jit(solution)/shard_map/dc,rce->dre/dot_general | solution.py:105
  41.9 1.6 %collective-permute-start.34 = (f32[8,1024]{1,0:T(8,128)S(1)}, f32[8,1024]{1,0:T(8,128)S(1)}, u32[]{:S(2)}, u32[]{:S(2)}) collective-permute-start(f32[8,1024]{1,0:T(8,128)S(1)} %fusion.15), channel_id=1, source_target_pairs={{0,1},{1,2},{2,3},{3,0},{4,5},{5,6},{6,7},{7,4},{8,9},{9,10},{10,1... | collective-permute-start | bytes 98312 | tf_op jit(solution)/shard_map/ppermute | solution.py:21
  43.5 2.6 %collective-permute-start.33 = (f32[8,1024]{1,0:T(8,128)S(1)}, f32[8,1024]{1,0:T(8,128)S(1)}, u32[]{:S(2)}, u32[]{:S(2)}) collective-permute-start(f32[8,1024]{1,0:T(8,128)S(1)} %fusion.15), channel_id=1, source_target_pairs={{0,2},{1,3},{2,0},{3,1},{4,6},{5,7},{6,4},{7,5},{8,10},{9,11},{10,... | collective-permute-start | bytes 98312 | tf_op jit(solution)/shard_map/ppermute | solution.py:21
  46.1 1.3 %collective-permute-start.32 = (f32[8,1024]{1,0:T(8,128)S(1)}, f32[8,1024]{1,0:T(8,128)S(1)}, u32[]{:S(2)}, u32[]{:S(2)}) collective-permute-start(f32[8,1024]{1,0:T(8,128)S(1)} %fusion.15), channel_id=1, source_target_pairs={{0,3},{1,0},{2,1},{3,2},{4,7},{5,4},{6,5},{7,6},{8,11},{9,8},{10,9... | collective-permute-start | bytes 98312 | tf_op jit(solution)/shard_map/ppermute | solution.py:21
  47.6 0.7 collective-permute-done.33
  48.3 1.7 %collective-permute-done.32 = f32[8,1024]{1,0:T(8,128)S(1)} collective-permute-done((f32[8,1024]{1,0:T(8,128)S(1)}, f32[8,1024]{1,0:T(8,128)S(1)}, u32[]{:S(2)}, u32[]{:S(2)}) %collective-permute-start.32) | collective-permute-done | bytes 32800 | tf_op jit(solution)/shard_map/ppermute | solution.py:21
  50.0 0.6 add_convert_fusion
  50.8 3.0 %collective-permute-done.5 = bf16[2048,64]{0,1:T(8,128)(2,1)S(1)} collective-permute-done((bf16[2048,64]{0,1:T(8,128)(2,1)S(1)}, bf16[2048,64]{0,1:T(8,128)(2,1)S(1)}, u32[]{:S(2)}, u32[]{:S(2)}) %collective-permute-start.5) | collective-permute-done | bytes 262176 | tf_op jit(solution)/shard_map/ppermute | solution.py:43
  54.2 4.2 %collective-permute-done.6 = bf16[1024,64]{0,1:T(8,128)(2,1)S(1)} collective-permute-done((bf16[1024,64]{0,1:T(8,128)(2,1)S(1)}, bf16[1024,64]{0,1:T(8,128)(2,1)S(1)}, u32[]{:S(2)}, u32[]{:S(2)}) %collective-permute-start.6) | collective-permute-done | bytes 131104 | tf_op jit(solution)/shard_map/ppermute | solution.py:44
  58.9 1.3 %collective-permute-done.7 = bf16[3072,64]{0,1:T(8,128)(2,1)S(1)} collective-permute-done((bf16[3072,64]{0,1:T(8,128)(2,1)S(1)}, bf16[3072,64]{0,1:T(8,128)(2,1)S(1)}, u32[]{:S(2)}, u32[]{:S(2)}) %collective-permute-start.7) | collective-permute-done | bytes 393248 | tf_op jit(solution)/shard_map/ppermute | solution.py:45
  61.1 0.7 collective-permute-start.10
  61.8 0.3 collective-permute-start.9
  62.1 2.8 %collective-permute-start.8 = (bf16[128,64]{0,1:T(8,128)(2,1)S(1)}, bf16[128,64]{0,1:T(8,128)(2,1)S(1)}, u32[]{:S(2)}, u32[]{:S(2)}) collective-permute-start(bf16[128,64]{0,1:T(8,128)(2,1)S(1)} %fusion.22), channel_id=1, source_target_pairs={{0,3},{1,0},{2,1},{3,2},{4,7},{5,4},{6,5},{7,6},{8,11},{9,8},{10,9... | collective-permute-start | bytes 49160 | tf_op jit(solution)/shard_map/ppermute | solution.py:26
  65.2 1.5 %collective-permute-done.10 = bf16[128,64]{0,1:T(8,128)(2,1)S(1)} collective-permute-done((bf16[128,64]{0,1:T(8,128)(2,1)S(1)}, bf16[128,64]{0,1:T(8,128)(2,1)S(1)}, u32[]{:S(2)}, u32[]{:S(2)}) %collective-permute-start.10) | collective-permute-done | bytes 16416 | tf_op jit(solution)/shard_map/ppermute | solution.py:26
  66.7 0.5 collective-permute-done.8
  67.4 1.2 %collective-permute-start.16 = (bf16[128,256]{0,1:T(8,128)(2,1)S(1)}, bf16[128,256]{0,1:T(8,128)(2,1)S(1)}, u32[]{:S(2)}, u32[]{:S(2)}) collective-permute-start(bf16[128,256]{0,1:T(8,128)(2,1)S(1)} %constant_dynamic-update-slice_fusion.1), channel_id=1, source_target_pairs={{0,24},{4,28},{8,0},{12,4},{16,8},{20,12},{24,16},{28,20},{1,25},{... | collective-permute-start | bytes 196616 | tf_op jit(solution)/shard_map/ppermute | solution.py:21
  68.6 0.8 collective-permute-start.15
  69.6 6.0 %collective-permute-done.1 = bf16[2048,256]{1,0:T(8,128)(2,1)S(1)} collective-permute-done((bf16[2048,256]{1,0:T(8,128)(2,1)S(1)}, bf16[2048,256]{1,0:T(8,128)(2,1)S(1)}, u32[]{:S(2)}, u32[]{:S(2)}) %collective-permute-start.1) | collective-permute-done | bytes 1048608 | tf_op jit(solution)/shard_map/ppermute | solution.py:43
  75.7 0.4 collective-permute-start.12
  76.0 5.5 %collective-permute-done.12 = bf16[128,256]{0,1:T(8,128)(2,1)S(1)} collective-permute-done((bf16[128,256]{0,1:T(8,128)(2,1)S(1)}, bf16[128,256]{0,1:T(8,128)(2,1)S(1)}, u32[]{:S(2)}, u32[]{:S(2)}) %collective-permute-start.12) | collective-permute-done | bytes 65568 | tf_op jit(solution)/shard_map/ppermute | solution.py:21
  81.6 0.6 collective-permute-start.14
  82.2 2.7 %collective-permute-done.2 = bf16[1024,256]{1,0:T(8,128)(2,1)S(1)} collective-permute-done((bf16[1024,256]{1,0:T(8,128)(2,1)S(1)}, bf16[1024,256]{1,0:T(8,128)(2,1)S(1)}, u32[]{:S(2)}, u32[]{:S(2)}) %collective-permute-start.2) | collective-permute-done | bytes 524320 | tf_op jit(solution)/shard_map/ppermute | solution.py:44
  84.9 0.8 collective-permute-start.13
  85.8 3.7 %collective-permute-done.13 = bf16[128,256]{0,1:T(8,128)(2,1)S(1)} collective-permute-done((bf16[128,256]{0,1:T(8,128)(2,1)S(1)}, bf16[128,256]{0,1:T(8,128)(2,1)S(1)}, u32[]{:S(2)}, u32[]{:S(2)}) %collective-permute-start.13) | collective-permute-done | bytes 65568 | tf_op jit(solution)/shard_map/ppermute | solution.py:21
  89.5 1.8 %collective-permute-start.3 = (bf16[3072,256]{1,0:T(8,128)(2,1)S(1)}, bf16[3072,256]{1,0:T(8,128)(2,1)S(1)}, u32[]{:S(2)}, u32[]{:S(2)}) collective-permute-start(bf16[3072,256]{1,0:T(8,128)(2,1)S(1)} %pad_maximum_fusion), channel_id=1, source_target_pairs={{0,4},{4,0},{8,12},{12,8},{16,20},{20,16},{24,28},{28,24},{1,5},{5... | collective-permute-start | bytes 4718600 | tf_op jit(solution)/shard_map/ppermute | solution.py:45
  91.5 0.2 fusion.29
  91.8 0.2 fusion.45
  92.0 2.4 %collective-permute-done.3 = bf16[3072,256]{1,0:T(8,128)(2,1)S(1)} collective-permute-done((bf16[3072,256]{1,0:T(8,128)(2,1)S(1)}, bf16[3072,256]{1,0:T(8,128)(2,1)S(1)}, u32[]{:S(2)}, u32[]{:S(2)}) %collective-permute-start.3) | collective-permute-done | bytes 1572896 | tf_op jit(solution)/shard_map/ppermute | solution.py:45
  94.6 0.2 fusion.25
  94.9 0.2 fusion.27
  95.1 0.2 fusion.16
  95.4 0.6 copy-done.8
  96.0 0.7 fusion.104
  96.7 1.3 %fusion.7 = f32[128,2,1024]{2,0,1:T(8,128)S(1)} fusion(pred[128,1024]{1,0:T(8,128)(4,1)S(1)} %copy-done.5, bf16[1024,128]{0,1:T(8,128)(2,1)} %copy-done.7, bf16[16,2,8,128]{3,2,1,0:T(8,128)(2,1)} %copy-done.8), kind=kOutput, calls=%fused_computation.12 | convolution fusion | flops 67633152 | bytes 1507328 | tf_op jit(solution)/shard_map/qhd,kd->qhk/dot_general | solution.py:156
  98.0 2.0 %fusion.14 = bf16[128,2,128]{0,2,1:T(8,128)(2,1)} fusion(bf16[1024,128]{0,1:T(8,128)(2,1)} %copy-done.11, f32[128,2,1024]{2,0,1:T(8,128)S(1)} %fusion.7, pred[128,1024]{1,0:T(8,128)(4,1)S(1)} %copy-done.5, f32[128,2]{0,1:T(2,128)S(1)} %fusion.104), kind=kOutput, calls=%fused_computation.23 | convolution fusion | flops 67962112 | bytes 1508352 | tf_op jit(solution)/shard_map/qhk,kd->qhd/dot_general | solution.py:163
  100.1 1.6 %copy.23 = bf16[128,256]{1,0:T(8,128)(2,1)} copy(bf16[128,256]{0,1:T(8,128)(2,1)} %bitcast.36) | data formatting | bytes 131072
  (104 shorter events, 3.9 us)
Async XLA Ops:
  0.6 24.7 %copy-start = (bf16[1024,1152]{1,0:T(8,128)(2,1)S(1)}, bf16[1024,1152]{1,0:T(8,128)(2,1)}, u32[]{:S(2)}) copy-start(bf16[1024,1152]{1,0:T(8,128)(2,1)} %param.15) | copy-start | bytes 7077892
  0.6 3.2 %copy-start.10 = (bf16[8192]{0:T(1024)(128)(2,1)S(1)}, bf16[8192]{0:T(1024)(128)(2,1)}, u32[]{:S(2)}) copy-start(bf16[8192]{0:T(1024)(128)(2,1)} %param.10) | copy-start | bytes 49156
  6.2 1.4 %copy-start.1 = (bf16[128,8192]{1,0:T(8,128)(2,1)}, bf16[128,8192]{1,0:T(8,128)(2,1)S(1)}, u32[]{:S(2)}) copy-start(bf16[128,8192]{1,0:T(8,128)(2,1)S(1)} %fusion.3) | copy-start | bytes 6291460
  6.2 10.3 %copy-start.3 = (bf16[1024,256]{1,0:T(8,128)(2,1)S(1)}, bf16[1024,256]{1,0:T(8,128)(2,1)}, u32[]{:S(2)}) copy-start(bf16[1024,256]{1,0:T(8,128)(2,1)} %param.11) | copy-start | bytes 1572868
  6.3 12.1 %copy-start.12 = (s32[8]{0:T(128)S(1)}, s32[8]{0:T(128)}, u32[]{:S(2)}) copy-start(s32[8]{0:T(128)} %param.17) | copy-start | bytes 100
  8.0 0.7 copy-start.4
  9.3 9.6 %collective-permute-start.18 = (bf16[8,1024]{1,0:T(8,128)(2,1)S(1)}, bf16[8,1024]{1,0:T(8,128)(2,1)S(1)}, u32[]{:S(2)}, u32[]{:S(2)}) collective-permute-start(bf16[8,1024]{1,0:T(8,128)(2,1)S(1)} %get-tuple-element.8), channel_id=1, source_target_pairs={{0,4},{4,8},{8,12},{12,16},{16,20},{20,24},{24,28},{28,0},{1,5},{5... | collective-permute-start | bytes 49160 | tf_op jit(solution)/shard_map/ppermute | solution.py:21
  9.8 10.5 %collective-permute-start.24 = (bf16[8,1024]{1,0:T(8,128)(2,1)S(1)}, bf16[8,1024]{1,0:T(8,128)(2,1)S(1)}, u32[]{:S(2)}, u32[]{:S(2)}) collective-permute-start(bf16[8,1024]{1,0:T(8,128)(2,1)S(1)} %get-tuple-element.9), channel_id=1, source_target_pairs={{0,28},{4,0},{8,4},{12,8},{16,12},{20,16},{24,20},{28,24},{1,29},{... | collective-permute-start | bytes 49160 | tf_op jit(solution)/shard_map/ppermute | solution.py:21
  12.7 11.5 %collective-permute-start.23 = (bf16[8,1024]{1,0:T(8,128)(2,1)}, bf16[8,1024]{1,0:T(8,128)(2,1)}, u32[]{:S(2)}, u32[]{:S(2)}) collective-permute-start(bf16[8,1024]{1,0:T(8,128)(2,1)} %get-tuple-element.10), channel_id=1, source_target_pairs={{0,24},{4,28},{8,0},{12,4},{16,8},{20,12},{24,16},{28,20},{1,25},{... | collective-permute-start | bytes 49160 | tf_op jit(solution)/shard_map/ppermute | solution.py:21
  15.0 9.3 %collective-permute-start.22 = (bf16[8,1024]{1,0:T(8,128)(2,1)}, bf16[8,1024]{1,0:T(8,128)(2,1)}, u32[]{:S(2)}, u32[]{:S(2)}) collective-permute-start(bf16[8,1024]{1,0:T(8,128)(2,1)} %get-tuple-element.11), channel_id=1, source_target_pairs={{0,20},{4,24},{8,28},{12,0},{16,4},{20,8},{24,12},{28,16},{1,21},{... | collective-permute-start | bytes 49160 | tf_op jit(solution)/shard_map/ppermute | solution.py:21
  15.0 9.3 %collective-permute-start.21 = (bf16[8,1024]{1,0:T(8,128)(2,1)}, bf16[8,1024]{1,0:T(8,128)(2,1)}, u32[]{:S(2)}, u32[]{:S(2)}) collective-permute-start(bf16[8,1024]{1,0:T(8,128)(2,1)} %get-tuple-element.12), channel_id=1, source_target_pairs={{0,16},{4,20},{8,24},{12,28},{16,0},{20,4},{24,8},{28,12},{1,17},{... | collective-permute-start | bytes 49160 | tf_op jit(solution)/shard_map/ppermute | solution.py:21
  18.9 5.4 %collective-permute-start.20 = (bf16[8,1024]{1,0:T(8,128)(2,1)}, bf16[8,1024]{1,0:T(8,128)(2,1)}, u32[]{:S(2)}, u32[]{:S(2)}) collective-permute-start(bf16[8,1024]{1,0:T(8,128)(2,1)} %get-tuple-element.13), channel_id=1, source_target_pairs={{0,12},{4,16},{8,20},{12,24},{16,28},{20,0},{24,4},{28,8},{1,13},{... | collective-permute-start | bytes 49160 | tf_op jit(solution)/shard_map/ppermute | solution.py:21
  20.3 3.6 %copy-start.9 = (bf16[8,1024]{1,0:T(8,128)(2,1)}, bf16[8,1024]{1,0:T(8,128)(2,1)S(1)}, u32[]{:S(2)}) copy-start(bf16[8,1024]{1,0:T(8,128)(2,1)S(1)} %collective-permute-done.24) | copy-start | bytes 49156
  20.3 5.0 %collective-permute-start.19 = (bf16[8,1024]{1,0:T(8,128)(2,1)}, bf16[8,1024]{1,0:T(8,128)(2,1)}, u32[]{:S(2)}, u32[]{:S(2)}) collective-permute-start(bf16[8,1024]{1,0:T(8,128)(2,1)} %get-tuple-element.14), channel_id=1, source_target_pairs={{0,8},{4,12},{8,16},{12,20},{16,24},{20,28},{24,0},{28,4},{1,9},{5... | collective-permute-start | bytes 49160 | tf_op jit(solution)/shard_map/ppermute | solution.py:21
  26.5 4.6 %collective-permute-start.31 = (f32[8,1152]{1,0:T(8,128)S(1)}, f32[8,1152]{1,0:T(8,128)S(1)}, u32[]{:S(2)}, u32[]{:S(2)}) collective-permute-start(f32[8,1152]{1,0:T(8,128)S(1)} %fusion.71), channel_id=1, source_target_pairs={{0,28},{4,0},{8,4},{12,8},{16,12},{20,16},{24,20},{28,24},{1,29},{... | collective-permute-start | bytes 110600 | tf_op jit(solution)/shard_map/ppermute | solution.py:21
  26.6 6.0 %collective-permute-start.30 = (f32[8,1152]{1,0:T(8,128)S(1)}, f32[8,1152]{1,0:T(8,128)S(1)}, u32[]{:S(2)}, u32[]{:S(2)}) collective-permute-start(f32[8,1152]{1,0:T(8,128)S(1)} %fusion.71), channel_id=1, source_target_pairs={{0,24},{4,28},{8,0},{12,4},{16,8},{20,12},{24,16},{28,20},{1,25},{... | collective-permute-start | bytes 110600 | tf_op jit(solution)/shard_map/ppermute | solution.py:21
  28.4 5.6 %collective-permute-start.29 = (f32[8,1152]{1,0:T(8,128)S(1)}, f32[8,1152]{1,0:T(8,128)S(1)}, u32[]{:S(2)}, u32[]{:S(2)}) collective-permute-start(f32[8,1152]{1,0:T(8,128)S(1)} %fusion.71), channel_id=1, source_target_pairs={{0,20},{4,24},{8,28},{12,0},{16,4},{20,8},{24,12},{28,16},{1,21},{... | collective-permute-start | bytes 110600 | tf_op jit(solution)/shard_map/ppermute | solution.py:21
  29.4 5.6 %collective-permute-start.28 = (f32[8,1152]{1,0:T(8,128)S(1)}, f32[8,1152]{1,0:T(8,128)S(1)}, u32[]{:S(2)}, u32[]{:S(2)}) collective-permute-start(f32[8,1152]{1,0:T(8,128)S(1)} %fusion.71), channel_id=1, source_target_pairs={{0,16},{4,20},{8,24},{12,28},{16,0},{20,4},{24,8},{28,12},{1,17},{... | collective-permute-start | bytes 110600 | tf_op jit(solution)/shard_map/ppermute | solution.py:21
  29.7 5.3 %collective-permute-start.27 = (f32[8,1152]{1,0:T(8,128)S(1)}, f32[8,1152]{1,0:T(8,128)S(1)}, u32[]{:S(2)}, u32[]{:S(2)}) collective-permute-start(f32[8,1152]{1,0:T(8,128)S(1)} %fusion.71), channel_id=1, source_target_pairs={{0,12},{4,16},{8,20},{12,24},{16,28},{20,0},{24,4},{28,8},{1,13},{... | collective-permute-start | bytes 110600 | tf_op jit(solution)/shard_map/ppermute | solution.py:21
  31.1 4.9 %collective-permute-start.26 = (f32[8,1152]{1,0:T(8,128)S(1)}, f32[8,1152]{1,0:T(8,128)S(1)}, u32[]{:S(2)}, u32[]{:S(2)}) collective-permute-start(f32[8,1152]{1,0:T(8,128)S(1)} %fusion.71), channel_id=1, source_target_pairs={{0,8},{4,12},{8,16},{12,20},{16,24},{20,28},{24,0},{28,4},{1,9},{5... | collective-permute-start | bytes 110600 | tf_op jit(solution)/shard_map/ppermute | solution.py:21
  32.6 4.3 %collective-permute-start.25 = (f32[8,1152]{1,0:T(8,128)S(1)}, f32[8,1152]{1,0:T(8,128)S(1)}, u32[]{:S(2)}, u32[]{:S(2)}) collective-permute-start(f32[8,1152]{1,0:T(8,128)S(1)} %fusion.71), channel_id=1, source_target_pairs={{0,4},{4,8},{8,12},{12,16},{16,20},{20,24},{24,28},{28,0},{1,5},{5... | collective-permute-start | bytes 110600 | tf_op jit(solution)/shard_map/ppermute | solution.py:21
  34.0 16.7 %copy-start.2 = (bf16[128,8192]{1,0:T(8,128)(2,1)S(1)}, bf16[128,8192]{1,0:T(8,128)(2,1)}, u32[]{:S(2)}) copy-start(bf16[128,8192]{1,0:T(8,128)(2,1)} %copy-done.1) | copy-start | bytes 6291460
  34.0 24.5 %collective-permute-start = (bf16[1024,256]{1,0:T(8,128)(2,1)S(1)}, bf16[1024,256]{1,0:T(8,128)(2,1)S(1)}, u32[]{:S(2)}, u32[]{:S(2)}) collective-permute-start(bf16[1024,256]{1,0:T(8,128)(2,1)S(1)} %copy-done.3), channel_id=1, source_target_pairs={{0,4},{4,0},{8,12},{12,8},{16,20},{20,16},{24,28},{28,24},{1,5},{5... | collective-permute-start | bytes 1572872 | tf_op jit(solution)/shard_map/ppermute | solution.py:41
  35.0 12.5 %collective-permute-start.4 = (bf16[1024,64]{0,1:T(8,128)(2,1)S(1)}, bf16[1024,64]{0,1:T(8,128)(2,1)S(1)}, u32[]{:S(2)}, u32[]{:S(2)}) collective-permute-start(bf16[1024,64]{0,1:T(8,128)(2,1)S(1)} %pad_maximum_fusion.4), channel_id=1, source_target_pairs={{0,4},{4,0},{8,12},{12,8},{16,20},{20,16},{24,28},{28,24},{1,5},{5... | collective-permute-start | bytes 393224 | tf_op jit(solution)/shard_map/ppermute | solution.py:41
  41.9 5.7 %collective-permute-start.34 = (f32[8,1024]{1,0:T(8,128)S(1)}, f32[8,1024]{1,0:T(8,128)S(1)}, u32[]{:S(2)}, u32[]{:S(2)}) collective-permute-start(f32[8,1024]{1,0:T(8,128)S(1)} %fusion.15), channel_id=1, source_target_pairs={{0,1},{1,2},{2,3},{3,0},{4,5},{5,6},{6,7},{7,4},{8,9},{9,10},{10,1... | collective-permute-start | bytes 98312 | tf_op jit(solution)/shard_map/ppermute | solution.py:21
  43.5 4.8 %collective-permute-start.33 = (f32[8,1024]{1,0:T(8,128)S(1)}, f32[8,1024]{1,0:T(8,128)S(1)}, u32[]{:S(2)}, u32[]{:S(2)}) collective-permute-start(f32[8,1024]{1,0:T(8,128)S(1)} %fusion.15), channel_id=1, source_target_pairs={{0,2},{1,3},{2,0},{3,1},{4,6},{5,7},{6,4},{7,5},{8,10},{9,11},{10,... | collective-permute-start | bytes 98312 | tf_op jit(solution)/shard_map/ppermute | solution.py:21
  46.1 3.9 %collective-permute-start.32 = (f32[8,1024]{1,0:T(8,128)S(1)}, f32[8,1024]{1,0:T(8,128)S(1)}, u32[]{:S(2)}, u32[]{:S(2)}) collective-permute-start(f32[8,1024]{1,0:T(8,128)S(1)} %fusion.15), channel_id=1, source_target_pairs={{0,3},{1,0},{2,1},{3,2},{4,7},{5,4},{6,5},{7,6},{8,11},{9,8},{10,9... | collective-permute-start | bytes 98312 | tf_op jit(solution)/shard_map/ppermute | solution.py:21
  47.5 6.4 %collective-permute-start.5 = (bf16[2048,64]{0,1:T(8,128)(2,1)S(1)}, bf16[2048,64]{0,1:T(8,128)(2,1)S(1)}, u32[]{:S(2)}, u32[]{:S(2)}) collective-permute-start(bf16[2048,64]{0,1:T(8,128)(2,1)S(1)} %pad_maximum_fusion.3), channel_id=1, source_target_pairs={{0,8},{4,20},{8,0},{12,28},{16,24},{20,4},{24,16},{28,12},{1,9},{5... | collective-permute-start | bytes 786440 | tf_op jit(solution)/shard_map/ppermute | solution.py:43
  53.9 4.4 %collective-permute-start.6 = (bf16[1024,64]{0,1:T(8,128)(2,1)S(1)}, bf16[1024,64]{0,1:T(8,128)(2,1)S(1)}, u32[]{:S(2)}, u32[]{:S(2)}) collective-permute-start(bf16[1024,64]{0,1:T(8,128)(2,1)S(1)} %slice.139), channel_id=1, source_target_pairs={{0,20},{4,8},{8,28},{12,0},{16,4},{20,24},{24,12},{28,16},{1,21},{... | collective-permute-start | bytes 393224 | tf_op jit(solution)/shard_map/ppermute | solution.py:44
  58.4 6.6 %copy-start.6 = (f32[128,256]{1,0:T(8,128)S(1)}, f32[128,256]{1,0:T(8,128)}, u32[]{:S(2)}) copy-start(f32[128,256]{1,0:T(8,128)} %fusion.56) | copy-start | bytes 393220
  58.4 1.8 %collective-permute-start.7 = (bf16[3072,64]{0,1:T(8,128)(2,1)S(1)}, bf16[3072,64]{0,1:T(8,128)(2,1)S(1)}, u32[]{:S(2)}, u32[]{:S(2)}) collective-permute-start(bf16[3072,64]{0,1:T(8,128)(2,1)S(1)} %pad_maximum_fusion.2), channel_id=1, source_target_pairs={{0,4},{4,0},{8,12},{12,8},{16,20},{20,16},{24,28},{28,24},{1,5},{5... | collective-permute-start | bytes 1179656 | tf_op jit(solution)/shard_map/ppermute | solution.py:45
  58.6 17.0 %collective-permute-start.1 = (bf16[2048,256]{1,0:T(8,128)(2,1)S(1)}, bf16[2048,256]{1,0:T(8,128)(2,1)S(1)}, u32[]{:S(2)}, u32[]{:S(2)}) collective-permute-start(bf16[2048,256]{1,0:T(8,128)(2,1)S(1)} %pad_maximum_fusion.1), channel_id=1, source_target_pairs={{0,8},{4,20},{8,0},{12,28},{16,24},{20,4},{24,16},{28,12},{1,9},{5... | collective-permute-start | bytes 3145736 | tf_op jit(solution)/shard_map/ppermute | solution.py:43
  61.1 5.6 %collective-permute-start.10 = (bf16[128,64]{0,1:T(8,128)(2,1)S(1)}, bf16[128,64]{0,1:T(8,128)(2,1)S(1)}, u32[]{:S(2)}, u32[]{:S(2)}) collective-permute-start(bf16[128,64]{0,1:T(8,128)(2,1)S(1)} %fusion.22), channel_id=1, source_target_pairs={{0,1},{1,2},{2,3},{3,0},{4,5},{5,6},{6,7},{7,4},{8,9},{9,10},{10,1... | collective-permute-start | bytes 49160 | tf_op jit(solution)/shard_map/ppermute | solution.py:26
  61.8 4.9 %collective-permute-start.9 = (bf16[128,64]{0,1:T(8,128)(2,1)S(1)}, bf16[128,64]{0,1:T(8,128)(2,1)S(1)}, u32[]{:S(2)}, u32[]{:S(2)}) collective-permute-start(bf16[128,64]{0,1:T(8,128)(2,1)S(1)} %fusion.22), channel_id=1, source_target_pairs={{0,2},{1,3},{2,0},{3,1},{4,6},{5,7},{6,4},{7,5},{8,10},{9,11},{10,... | collective-permute-start | bytes 49160 | tf_op jit(solution)/shard_map/ppermute | solution.py:26
  62.1 5.1 %collective-permute-start.8 = (bf16[128,64]{0,1:T(8,128)(2,1)S(1)}, bf16[128,64]{0,1:T(8,128)(2,1)S(1)}, u32[]{:S(2)}, u32[]{:S(2)}) collective-permute-start(bf16[128,64]{0,1:T(8,128)(2,1)S(1)} %fusion.22), channel_id=1, source_target_pairs={{0,3},{1,0},{2,1},{3,2},{4,7},{5,4},{6,5},{7,6},{8,11},{9,8},{10,9... | collective-permute-start | bytes 49160 | tf_op jit(solution)/shard_map/ppermute | solution.py:26
  67.4 24.1 %collective-permute-start.17 = (bf16[128,256]{0,1:T(8,128)(2,1)S(1)}, bf16[128,256]{0,1:T(8,128)(2,1)S(1)}, u32[]{:S(2)}, u32[]{:S(2)}) collective-permute-start(bf16[128,256]{0,1:T(8,128)(2,1)S(1)} %constant_dynamic-update-slice_fusion.1), channel_id=1, source_target_pairs={{0,28},{4,0},{8,4},{12,8},{16,12},{20,16},{24,20},{28,24},{1,29},{... | collective-permute-start | bytes 196616 | tf_op jit(solution)/shard_map/ppermute | solution.py:21
  67.4 24.0 %collective-permute-start.16 = (bf16[128,256]{0,1:T(8,128)(2,1)S(1)}, bf16[128,256]{0,1:T(8,128)(2,1)S(1)}, u32[]{:S(2)}, u32[]{:S(2)}) collective-permute-start(bf16[128,256]{0,1:T(8,128)(2,1)S(1)} %constant_dynamic-update-slice_fusion.1), channel_id=1, source_target_pairs={{0,24},{4,28},{8,0},{12,4},{16,8},{20,12},{24,16},{28,20},{1,25},{... | collective-permute-start | bytes 196616 | tf_op jit(solution)/shard_map/ppermute | solution.py:21
  68.6 22.8 %collective-permute-start.15 = (bf16[128,256]{0,1:T(8,128)(2,1)S(1)}, bf16[128,256]{0,1:T(8,128)(2,1)S(1)}, u32[]{:S(2)}, u32[]{:S(2)}) collective-permute-start(bf16[128,256]{0,1:T(8,128)(2,1)S(1)} %constant_dynamic-update-slice_fusion.1), channel_id=1, source_target_pairs={{0,20},{4,24},{8,28},{12,0},{16,4},{20,8},{24,12},{28,16},{1,21},{... | collective-permute-start | bytes 196616 | tf_op jit(solution)/shard_map/ppermute | solution.py:21
  69.4 6.2 %collective-permute-start.11 = (bf16[128,256]{0,1:T(8,128)(2,1)S(1)}, bf16[128,256]{0,1:T(8,128)(2,1)S(1)}, u32[]{:S(2)}, u32[]{:S(2)}) collective-permute-start(bf16[128,256]{0,1:T(8,128)(2,1)S(1)} %constant_dynamic-update-slice_fusion.1), channel_id=1, source_target_pairs={{0,4},{4,8},{8,12},{12,16},{16,20},{20,24},{24,28},{28,0},{1,5},{5... | collective-permute-start | bytes 196616 | tf_op jit(solution)/shard_map/ppermute | solution.py:21
  75.6 9.4 %collective-permute-start.2 = (bf16[1024,256]{1,0:T(8,128)(2,1)S(1)}, bf16[1024,256]{1,0:T(8,128)(2,1)S(1)}, u32[]{:S(2)}, u32[]{:S(2)}) collective-permute-start(bf16[1024,256]{1,0:T(8,128)(2,1)S(1)} %slice.134), channel_id=1, source_target_pairs={{0,20},{4,8},{8,28},{12,0},{16,4},{20,24},{24,12},{28,16},{1,21},{... | collective-permute-start | bytes 1572872 | tf_op jit(solution)/shard_map/ppermute | solution.py:44
  75.7 5.9 %collective-permute-start.12 = (bf16[128,256]{0,1:T(8,128)(2,1)S(1)}, bf16[128,256]{0,1:T(8,128)(2,1)S(1)}, u32[]{:S(2)}, u32[]{:S(2)}) collective-permute-start(bf16[128,256]{0,1:T(8,128)(2,1)S(1)} %constant_dynamic-update-slice_fusion.1), channel_id=1, source_target_pairs={{0,8},{4,12},{8,16},{12,20},{16,24},{20,28},{24,0},{28,4},{1,9},{5... | collective-permute-start | bytes 196616 | tf_op jit(solution)/shard_map/ppermute | solution.py:21
  81.6 9.8 %collective-permute-start.14 = (bf16[128,256]{0,1:T(8,128)(2,1)S(1)}, bf16[128,256]{0,1:T(8,128)(2,1)S(1)}, u32[]{:S(2)}, u32[]{:S(2)}) collective-permute-start(bf16[128,256]{0,1:T(8,128)(2,1)S(1)} %constant_dynamic-update-slice_fusion.1), channel_id=1, source_target_pairs={{0,16},{4,20},{8,24},{12,28},{16,0},{20,4},{24,8},{28,12},{1,17},{... | collective-permute-start | bytes 196616 | tf_op jit(solution)/shard_map/ppermute | solution.py:21
  84.9 4.6 %collective-permute-start.13 = (bf16[128,256]{0,1:T(8,128)(2,1)S(1)}, bf16[128,256]{0,1:T(8,128)(2,1)S(1)}, u32[]{:S(2)}, u32[]{:S(2)}) collective-permute-start(bf16[128,256]{0,1:T(8,128)(2,1)S(1)} %constant_dynamic-update-slice_fusion.1), channel_id=1, source_target_pairs={{0,12},{4,16},{8,20},{12,24},{16,28},{20,0},{24,4},{28,8},{1,13},{... | collective-permute-start | bytes 196616 | tf_op jit(solution)/shard_map/ppermute | solution.py:21
  89.5 4.9 %collective-permute-start.3 = (bf16[3072,256]{1,0:T(8,128)(2,1)S(1)}, bf16[3072,256]{1,0:T(8,128)(2,1)S(1)}, u32[]{:S(2)}, u32[]{:S(2)}) collective-permute-start(bf16[3072,256]{1,0:T(8,128)(2,1)S(1)} %pad_maximum_fusion), channel_id=1, source_target_pairs={{0,4},{4,0},{8,12},{12,8},{16,20},{20,16},{24,28},{28,24},{1,5},{5... | collective-permute-start | bytes 4718600 | tf_op jit(solution)/shard_map/ppermute | solution.py:45
  91.5 3.6 %copy-start.11 = (bf16[1024,128]{0,1:T(8,128)(2,1)}, bf16[1024,128]{0,1:T(8,128)(2,1)S(1)}, u32[]{:S(2)}) copy-start(bf16[1024,128]{0,1:T(8,128)(2,1)S(1)} %get-tuple-element.16) | copy-start | bytes 786436
  91.5 3.9 %copy-start.7 = (bf16[1024,128]{0,1:T(8,128)(2,1)}, bf16[1024,128]{0,1:T(8,128)(2,1)S(1)}, u32[]{:S(2)}) copy-start(bf16[1024,128]{0,1:T(8,128)(2,1)S(1)} %get-tuple-element.15) | copy-start | bytes 786436
  92.0 4.0 %copy-start.5 = (pred[128,1024]{1,0:T(8,128)(4,1)S(1)}, pred[128,1024]{1,0:T(8,128)(4,1)}, u32[]{:S(2)}) copy-start(pred[128,1024]{1,0:T(8,128)(4,1)} %compare_and_fusion) | copy-start | bytes 393220
  95.4 0.6 copy-start.8
